TPU v7x, 32 devices: a whole 2x2x4 slice. The times are simulated.
32 devices in a mesh: ctx: 4 (over x, core), ep: 8 (over z, y).
Axes of the slice: x: 2, y: 2, z: 4, core: 2. Of those that a mesh axis runs over, the one named last changes fastest.
Arguments:
- query_latent: bfloat16 [1, 512, 128, 512], P(None, 'ctx', 'ep'), may hold values from -6 to 6
- query_rope: bfloat16 [1, 128, 64, 512], P(None, 'ep', None, 'ctx'), may hold values from -12 to 12
- key_latent: bfloat16 [1, 512, 512], P(None, 'ctx'), may hold values from -6 to 6
- key_rope: bfloat16 [1, 64, 512], P(None, None, 'ctx'), may hold values from -14 to 14
- output_grad: bfloat16 [1, 512, 128, 512], P(None, 'ctx', 'ep'), may hold values from -6 to 6
Outputs:
- attended: bfloat16 [1, 512, 128, 512], P(None, 'ctx', 'ep')
- query_latent_grad: bfloat16 [1, 512, 128, 512], P(None, 'ctx', 'ep')
- query_rope_grad: bfloat16 [1, 128, 64, 512], P(None, 'ep', None, 'ctx')
- key_latent_grad: bfloat16 [1, 512, 512], P(None, 'ctx')
- key_rope_grad: bfloat16 [1, 64, 512], P(None, None, 'ctx')
All inputs are finite; a program needn't handle non-finite values.
Results may differ from a plain program's by a relative error of at most 0.018.
Values may be sent and summed in bfloat16 or wider, within the bound.
No kernel may reach another device: no remote copies, remote signals or barrier semaphores. Data moves between devices by JAX's collectives and lax.ppermute only.
A program may use at most 64 MiB of HBM per device.

v0:
```python
import jax
import jax.numpy as jnp
from jax import lax
from jax.sharding import PartitionSpec as P

scale_factor = 192.0 ** (-0.5)


def causal_reduce_ctx(blocks, n_ctx):
    here = lax.axis_index("ctx")
    total = jnp.take(blocks, here, axis=0).astype(jnp.float32)
    for shift in range(1, n_ctx):
        sent = jnp.take(blocks, jnp.maximum(here - shift, 0), axis=0)
        got = lax.ppermute(sent, "ctx", [(i, i - shift) for i in range(shift, n_ctx)])
        total = total + got.astype(jnp.float32)
    return total


def butterfly_sum_ep(total, n_ep):
    if n_ep & n_ep - 1:
        return lax.psum(total.astype(jnp.bfloat16), "ep").astype(jnp.float32)
    bit = 1
    while bit < n_ep:
        mine = total.astype(jnp.bfloat16)
        theirs = lax.ppermute(mine, "ep", [(i, i ^ bit) for i in range(n_ep)])
        total = mine.astype(jnp.float32) + theirs.astype(jnp.float32)
        bit *= 2
    return total


def body(query_latent, query_rope, key_latent, key_rope, output_grad):
    n_ctx = lax.axis_size("ctx")
    n_ep = lax.axis_size("ep")
    block_len = query_latent.shape[1]
    kvr = key_latent.shape[2]
    local_keys = jnp.concatenate([key_latent[0], key_rope[0].T], axis=1)
    whole_keys = lax.all_gather(local_keys, "ctx", axis=0, tiled=True)
    whole_latent = whole_keys[None, :, :kvr]
    whole_rope = whole_keys[:, kvr:].T[None]
    length = whole_latent.shape[1]
    offset = lax.axis_index("ctx") * block_len
    query_place = offset + jnp.arange(block_len, dtype=jnp.int32)
    allowed = jnp.arange(length, dtype=jnp.int32)[None, :] <= query_place[:, None]
    scores = jnp.einsum(
        "sthd,sjd->shtj", query_latent, whole_latent, preferred_element_type=jnp.float32
    )
    scores = scores + jnp.einsum(
        "shdt,sdj->shtj", query_rope, whole_rope, preferred_element_type=jnp.float32
    )
    scores = jnp.where(allowed, scores * scale_factor, jnp.float32(-1e30))
    row_max = jnp.max(scores, axis=-1, keepdims=True)
    powers = jnp.exp(scores - row_max)
    weights = powers / jnp.sum(powers, axis=-1, keepdims=True)
    rounded_weights = weights.astype(jnp.bfloat16)
    attended = jnp.einsum(
        "shtj,sjd->sthd", rounded_weights, whole_latent, preferred_element_type=jnp.float32
    ).astype(jnp.bfloat16)
    row_dots = jnp.einsum(
        "sthd,sthd->sht", output_grad, attended, preferred_element_type=jnp.float32
    )
    weight_grad = jnp.einsum(
        "sthd,sjd->shtj", output_grad, whole_latent, preferred_element_type=jnp.float32
    )
    score_grad = (weights * (weight_grad - row_dots[..., None])).astype(jnp.bfloat16)
    latent_qgrad = (
        scale_factor
        * jnp.einsum("shtj,sjd->sthd", score_grad, whole_latent, preferred_element_type=jnp.float32)
    ).astype(jnp.bfloat16)
    rope_qgrad = (
        scale_factor
        * jnp.einsum("shtj,sdj->shdt", score_grad, whole_rope, preferred_element_type=jnp.float32)
    ).astype(jnp.bfloat16)
    latent_term = scale_factor * jnp.einsum(
        "shtj,sthd->jd", score_grad, query_latent, preferred_element_type=jnp.float32
    )
    latent_term = latent_term + jnp.einsum(
        "shtj,sthd->jd", rounded_weights, output_grad, preferred_element_type=jnp.float32
    )
    rope_term = scale_factor * jnp.einsum(
        "shtj,shdt->jd", score_grad, query_rope, preferred_element_type=jnp.float32
    )
    terms = jnp.concatenate([latent_term, rope_term], axis=1).astype(jnp.bfloat16)
    total = causal_reduce_ctx(terms.reshape(n_ctx, block_len, -1), n_ctx)
    total = butterfly_sum_ep(total, n_ep).astype(jnp.bfloat16)
    latent_kgrad = total[None, :, :kvr]
    rope_kgrad = total[:, kvr:].T[None]
    return (attended, latent_qgrad, rope_qgrad, latent_kgrad, rope_kgrad)


def solution(mesh):
    placed = (
        P(None, "ctx", "ep", None),
        P(None, "ep", None, "ctx"),
        P(None, "ctx", None),
        P(None, None, "ctx"),
        P(None, "ctx", "ep", None),
    )
    return jax.shard_map(
        body,
        mesh=mesh,
        in_specs=placed,
        out_specs=(
            P(None, "ctx", "ep", None),
            P(None, "ctx", "ep", None),
            P(None, "ep", None, "ctx"),
            P(None, "ctx", None),
            P(None, None, "ctx"),
        ),
        check_vma=False,
    )
```

profile of v0, /device:TPU:0, one launch (start us, length us, event | category | flops | bytes accessed | tf_op | source)
XLA Modules:
  0.0 93.7 jit_solution(13140443794704222318)
XLA Ops:
  0.6 1.0 %copy.27 = bf16[1,64,128]{1,2,0:T(8,128)(2,1)S(1)} copy(bf16[1,64,128]{2,1,0:T(8,128)(2,1)} %param.10) | data formatting | bytes 32768 | tf_op args[3]
  1.6 0.9 pad_maximum_fusion
  2.6 9.3 %all_gather.3 = bf16[512,576]{1,0:T(8,128)(2,1)S(1)} all-gather(bf16[128,576]{1,0:T(8,128)(2,1)S(1)} %pad_maximum_fusion), channel_id=1, replica_groups=mesh['ctx'=4,'ep'=8] {'ctx'}, dimensions={0}, use_global_device_ids=true | all-gather | bytes 737280 | tf_op jit(solution)/shard_map/all_gather | solution.py:37
  12.0 2.8 %fusion.23 = f32[512,128,16]{1,0,2:T(8,128)S(1)} fusion(bf16[128,16,512]{2,1,0:T(8,128)(2,1)S(1)} %bitcast.145, bf16[512,576]{1,0:T(8,128)(2,1)S(1)} %all_gather.3), kind=kOutput, calls=%fused_computation.27 | convolution fusion | flops 1073741824 | bytes 6815744 | tf_op jit(solution)/shard_map/sthd,sjd->shtj/dot_general | solution.py:44
  14.8 0.9 fusion.88
  15.7 0.6 fusion.5
  16.3 4.1 %bitcast_convert_fusion = (f32[16,128,512]{1,2,0:T(8,128)}, bf16[512,16,128]{2,0,1:T(8,128)(2,1)}) fusion(f32[16,128]{1,0:T(8,128)S(1)} %fusion.5, f32[1,16,128,512]{2,3,1,0:T(8,128)S(1)} %get-tuple-element.31, f32[16,128]{1,0:T(8,128)S(1)} %get-tuple-element.30, bf16[512,576]{1,0:T(8,128)(2,1)S(1)} %all_gather.3), kind=kOutput, calls=%fused_computation.18 | convolution fusion | flops 1078984704 | bytes 11026432 | tf_op jit(solution)/shard_map/shtj,sjd->sthd/dot_general | solution.py:55
  20.4 5.5 %copy.52 = f32[16,128,512]{2,0,1:T(8,128)} copy(f32[16,128,512]{1,2,0:T(8,128)} %get-tuple-element.32) | data formatting | bytes 8388608
  25.9 3.3 %multiply_reduce_fusion = f32[16,128]{0,1:T(8,128)S(1)} fusion(f32[16,128,512]{2,0,1:T(8,128)} %copy.52, bf16[1,128,16,512]{3,2,1,0:T(8,128)(2,1)} %param.11), kind=kLoop, calls=%fused_computation.6 | loop fusion | flops 3143680 | bytes 6299648
  29.3 6.8 %fusion.28 = f32[512,512]{1,0:T(8,128)} fusion(bf16[128,16,512]{2,1,0:T(8,128)(2,1)} %bitcast.147, f32[16,128]{1,0:T(8,128)S(1)} %fusion.5, f32[1,16,128,512]{2,3,1,0:T(8,128)} %copy-done.1, f32[16,128]{1,0:T(8,128)S(1)} %get-tuple-element.30), kind=kOutput, calls=%fused_computation.30 | convolution fusion | flops 1076887552 | bytes 7356416 | tf_op jit(solution)/shard_map/shtj,sthd->jd/dot_general | solution.py:76
  36.1 4.7 %fusion.1 = bf16[1,16,128,512]{2,3,1,0:T(8,128)(2,1)} fusion(f32[16,128]{1,0:T(8,128)S(1)} %copy.53, bf16[128,16,512]{2,1,0:T(8,128)(2,1)S(1)} %bitcast.148, f32[16,128]{1,0:T(8,128)S(1)} %fusion.5, f32[1,16,128,512]{2,3,1,0:T(8,128)S(1)} %copy-done.2, f32[16,128]{1,0:T(8,128)S(1)} %get-tuple-element.30, bf16[512,576]{1,0:T(8,128)(2,1)S(1)} %all_gather.3), kind=kOutput, calls=%fused_computation.2 | convolution fusion | flops 1078984704 | bytes 8937472 | tf_op jit(solution)/shard_map/sthd,sjd->shtj/dot_general | solution.py:61
  40.8 2.3 %fusion.69 = bf16[512,64]{0,1:T(8,128)(2,1)S(1)} fusion(bf16[1,16,128,512]{2,3,1,0:T(8,128)(2,1)} %fusion.1, bf16[1,16,64,128]{3,2,1,0:T(8,128)(2,1)S(1)} %copy-done.4), kind=kOutput, calls=%fused_computation.45 | convolution fusion | flops 134283264 | bytes 2424832 | tf_op jit(solution)/shard_map/shtj,shdt->jd/dot_general | solution.py:79
  43.2 4.4 %fusion.48 = bf16[512,512]{1,0:T(8,128)(2,1)S(1)} fusion(f32[512,512]{1,0:T(8,128)} %fusion.28, bf16[128,16,512]{2,1,0:T(8,128)(2,1)S(1)} %bitcast.146, bf16[1,16,128,512]{2,3,1,0:T(8,128)(2,1)} %fusion.1), kind=kOutput, calls=%fused_computation.34 | convolution fusion | flops 1074528256 | bytes 5767168 | tf_op jit(solution)/shard_map/shtj,sthd->jd/dot_general | solution.py:73
  47.6 0.1 copy.63
  47.7 0.8 fusion.82
  48.6 1.3 %collective-permute-start.2 = (bf16[128,576]{1,0:T(8,128)(2,1)}, bf16[128,576]{1,0:T(8,128)(2,1)}, u32[]{:S(2)}, u32[]{:S(2)}) collective-permute-start(bf16[128,576]{1,0:T(8,128)(2,1)} %get-tuple-element.29), channel_id=1, source_target_pairs={{24,0},{25,1},{26,2},{27,3},{28,4},{29,5},{30,6},{31,7}} | collective-permute-start | bytes 442376 | tf_op jit(solution)/shard_map/ppermute | solution.py:14
  49.9 1.3 %collective-permute-start.1 = (bf16[128,576]{1,0:T(8,128)(2,1)}, bf16[128,576]{1,0:T(8,128)(2,1)}, u32[]{:S(2)}, u32[]{:S(2)}) collective-permute-start(bf16[128,576]{1,0:T(8,128)(2,1)} %get-tuple-element.28), channel_id=1, source_target_pairs={{16,0},{24,8},{17,1},{25,9},{18,2},{26,10},{19,3},{27,11},{20,4},{... | collective-permute-start | bytes 442376 | tf_op jit(solution)/shard_map/ppermute | solution.py:14
  51.2 1.3 %collective-permute-start = (bf16[128,576]{1,0:T(8,128)(2,1)}, bf16[128,576]{1,0:T(8,128)(2,1)}, u32[]{:S(2)}, u32[]{:S(2)}) collective-permute-start(bf16[128,576]{1,0:T(8,128)(2,1)} %get-tuple-element.27), channel_id=1, source_target_pairs={{8,0},{16,8},{24,16},{9,1},{17,9},{25,17},{10,2},{18,10},{26,18},{... | collective-permute-start | bytes 442376 | tf_op jit(solution)/shard_map/ppermute | solution.py:14
  52.5 3.0 %collective-permute-done.2 = bf16[128,576]{1,0:T(8,128)(2,1)} collective-permute-done((bf16[128,576]{1,0:T(8,128)(2,1)}, bf16[128,576]{1,0:T(8,128)(2,1)}, u32[]{:S(2)}, u32[]{:S(2)}) %collective-permute-start.2) | collective-permute-done | bytes 147488 | tf_op jit(solution)/shard_map/ppermute | solution.py:14
  55.5 3.6 %collective-permute-done.1 = bf16[128,576]{1,0:T(8,128)(2,1)} collective-permute-done((bf16[128,576]{1,0:T(8,128)(2,1)}, bf16[128,576]{1,0:T(8,128)(2,1)}, u32[]{:S(2)}, u32[]{:S(2)}) %collective-permute-start.1) | collective-permute-done | bytes 147488 | tf_op jit(solution)/shard_map/ppermute | solution.py:14
  59.1 1.2 %add_convert_fusion.3 = bf16[128,576]{1,0:T(8,128)(2,1)S(1)} fusion(bf16[128,576]{1,0:T(8,128)(2,1)} %collective-permute-done.2, bf16[128,576]{1,0:T(8,128)(2,1)} %collective-permute-done.1, bf16[128,576]{1,0:T(8,128)(2,1)} %collective-permute-done, s32[]{:T(128)S(6)} %select_n.22, bf16[4,128,512]{2,1,0:T(8,128)(2,1)S(1)} %bitcast.151, ...), kind=kLoop, calls=%fused_computation.54 | loop fusion | flops 958464 | bytes 1179653 | tf_op jit(solution)/shard_map/convert_element_type | solution.py:24
  60.3 1.6 %collective-permute-start.3 = (bf16[128,576]{1,0:T(8,128)(2,1)S(1)}, bf16[128,576]{1,0:T(8,128)(2,1)S(1)}, u32[]{:S(2)}, u32[]{:S(2)}) collective-permute-start(bf16[128,576]{1,0:T(8,128)(2,1)S(1)} %add_convert_fusion.3), channel_id=1, source_target_pairs={{0,1},{1,0},{2,3},{3,2},{4,5},{5,4},{6,7},{7,6},{8,9},{9,8},{10,11... | collective-permute-start | bytes 442376 | tf_op jit(solution)/shard_map/ppermute | solution.py:25
  61.9 4.9 %collective-permute-done.3 = bf16[128,576]{1,0:T(8,128)(2,1)S(1)} collective-permute-done((bf16[128,576]{1,0:T(8,128)(2,1)S(1)}, bf16[128,576]{1,0:T(8,128)(2,1)S(1)}, u32[]{:S(2)}, u32[]{:S(2)}) %collective-permute-start.3) | collective-permute-done | bytes 147488 | tf_op jit(solution)/shard_map/ppermute | solution.py:25
  66.8 1.6 %collective-permute-start.4 = (bf16[128,576]{1,0:T(8,128)(2,1)S(1)}, bf16[128,576]{1,0:T(8,128)(2,1)S(1)}, u32[]{:S(2)}, u32[]{:S(2)}) collective-permute-start(bf16[128,576]{1,0:T(8,128)(2,1)S(1)} %add_convert_fusion.2), channel_id=1, source_target_pairs={{0,2},{1,3},{2,0},{3,1},{4,6},{5,7},{6,4},{7,5},{8,10},{9,11},{10,... | collective-permute-start | bytes 442376 | tf_op jit(solution)/shard_map/ppermute | solution.py:25
  68.5 4.2 %fusion.25 = bf16[1,128,16,512]{1,3,2,0:T(8,128)(2,1)} fusion(bf16[1,16,128,512]{2,3,1,0:T(8,128)(2,1)} %fusion.1, bf16[512,576]{1,0:T(8,128)(2,1)S(1)} %all_gather.3), kind=kOutput, calls=%fused_computation.29 | convolution fusion | flops 1075838976 | bytes 4718592 | tf_op jit(solution)/shard_map/shtj,sjd->sthd/dot_general | solution.py:67
  72.7 4.5 %copy.41 = bf16[1,128,16,512]{3,2,1,0:T(8,128)(2,1)} copy(bf16[1,128,16,512]{1,3,2,0:T(8,128)(2,1)} %bitcast.149) | data formatting | bytes 4194304
  77.2 4.5 %copy.42 = bf16[1,128,16,512]{3,2,1,0:T(8,128)(2,1)} copy(bf16[1,128,16,512]{1,3,2,0:T(8,128)(2,1)} %fusion.25) | data formatting | bytes 4194304
  81.7 2.6 %collective-permute-start.5 = (bf16[128,576]{1,0:T(8,128)(2,1)S(1)}, bf16[128,576]{1,0:T(8,128)(2,1)S(1)}, u32[]{:S(2)}, u32[]{:S(2)}) collective-permute-start(bf16[128,576]{1,0:T(8,128)(2,1)S(1)} %add_convert_fusion.1), channel_id=1, source_target_pairs={{0,4},{1,5},{2,6},{3,7},{4,0},{5,1},{6,2},{7,3},{8,12},{9,13},{10,... | collective-permute-start | bytes 442376 | tf_op jit(solution)/shard_map/ppermute | solution.py:25
  84.3 2.8 %fusion.60 = bf16[1,16,64,128]{3,2,1,0:T(8,128)(2,1)} fusion(bf16[1,16,128,512]{2,3,1,0:T(8,128)(2,1)} %fusion.1, bf16[512,576]{1,0:T(8,128)(2,1)S(1)} %all_gather.3), kind=kOutput, calls=%fused_computation.42 | convolution fusion | flops 134479872 | bytes 2490368 | tf_op jit(solution)/shard_map/shtj,sdj->shdt/dot_general | solution.py:71
  87.1 5.2 %collective-permute-done.5 = bf16[128,576]{1,0:T(8,128)(2,1)S(1)} collective-permute-done((bf16[128,576]{1,0:T(8,128)(2,1)S(1)}, bf16[128,576]{1,0:T(8,128)(2,1)S(1)}, u32[]{:S(2)}, u32[]{:S(2)}) %collective-permute-start.5) | collective-permute-done | bytes 147488 | tf_op jit(solution)/shard_map/ppermute | solution.py:25
  92.4 0.7 slice_bitcast_fusion.5
  93.0 0.7 copy.43
  (19 shorter events, 0.3 us)
Async XLA Ops:
  0.6 11.3 %copy-start = (bf16[1,128,16,512]{3,2,1,0:T(8,128)(2,1)S(1)}, bf16[1,128,16,512]{3,2,1,0:T(8,128)(2,1)}, u32[]{:S(2)}) copy-start(bf16[1,128,16,512]{3,2,1,0:T(8,128)(2,1)} %param.7) | copy-start | bytes 6291460
  12.0 2.8 %copy-start.4 = (bf16[1,16,64,128]{3,2,1,0:T(8,128)(2,1)S(1)}, bf16[1,16,64,128]{3,2,1,0:T(8,128)(2,1)}, u32[]{:S(2)}) copy-start(bf16[1,16,64,128]{3,2,1,0:T(8,128)(2,1)} %param.8) | copy-start | bytes 786436
  15.7 4.7 %copy-start.1 = (f32[1,16,128,512]{2,3,1,0:T(8,128)}, f32[1,16,128,512]{2,3,1,0:T(8,128)S(1)}, u32[]{:S(2)}) copy-start(f32[1,16,128,512]{2,3,1,0:T(8,128)S(1)} %get-tuple-element.31) | copy-start | bytes 12582916
  29.3 6.8 %copy-start.2 = (f32[1,16,128,512]{2,3,1,0:T(8,128)S(1)}, f32[1,16,128,512]{2,3,1,0:T(8,128)}, u32[]{:S(2)}) copy-start(f32[1,16,128,512]{2,3,1,0:T(8,128)} %copy-done.1) | copy-start | bytes 12582916
  29.3 6.8 %copy-start.3 = (bf16[1,128,16,512]{3,2,1,0:T(8,128)(2,1)S(1)}, bf16[1,128,16,512]{3,2,1,0:T(8,128)(2,1)}, u32[]{:S(2)}) copy-start(bf16[1,128,16,512]{3,2,1,0:T(8,128)(2,1)} %param.11) | copy-start | bytes 6291460
  48.6 6.9 %collective-permute-start.2 = (bf16[128,576]{1,0:T(8,128)(2,1)}, bf16[128,576]{1,0:T(8,128)(2,1)}, u32[]{:S(2)}, u32[]{:S(2)}) collective-permute-start(bf16[128,576]{1,0:T(8,128)(2,1)} %get-tuple-element.29), channel_id=1, source_target_pairs={{24,0},{25,1},{26,2},{27,3},{28,4},{29,5},{30,6},{31,7}} | collective-permute-start | bytes 442376 | tf_op jit(solution)/shard_map/ppermute | solution.py:14
  49.9 9.2 %collective-permute-start.1 = (bf16[128,576]{1,0:T(8,128)(2,1)}, bf16[128,576]{1,0:T(8,128)(2,1)}, u32[]{:S(2)}, u32[]{:S(2)}) collective-permute-start(bf16[128,576]{1,0:T(8,128)(2,1)} %get-tuple-element.28), channel_id=1, source_target_pairs={{16,0},{24,8},{17,1},{25,9},{18,2},{26,10},{19,3},{27,11},{20,4},{... | collective-permute-start | bytes 442376 | tf_op jit(solution)/shard_map/ppermute | solution.py:14
  51.2 7.9 %collective-permute-start = (bf16[128,576]{1,0:T(8,128)(2,1)}, bf16[128,576]{1,0:T(8,128)(2,1)}, u32[]{:S(2)}, u32[]{:S(2)}) collective-permute-start(bf16[128,576]{1,0:T(8,128)(2,1)} %get-tuple-element.27), channel_id=1, source_target_pairs={{8,0},{16,8},{24,16},{9,1},{17,9},{25,17},{10,2},{18,10},{26,18},{... | collective-permute-start | bytes 442376 | tf_op jit(solution)/shard_map/ppermute | solution.py:14
  60.3 6.5 %collective-permute-start.3 = (bf16[128,576]{1,0:T(8,128)(2,1)S(1)}, bf16[128,576]{1,0:T(8,128)(2,1)S(1)}, u32[]{:S(2)}, u32[]{:S(2)}) collective-permute-start(bf16[128,576]{1,0:T(8,128)(2,1)S(1)} %add_convert_fusion.3), channel_id=1, source_target_pairs={{0,1},{1,0},{2,3},{3,2},{4,5},{5,4},{6,7},{7,6},{8,9},{9,8},{10,11... | collective-permute-start | bytes 442376 | tf_op jit(solution)/shard_map/ppermute | solution.py:25
  66.8 14.8 %collective-permute-start.4 = (bf16[128,576]{1,0:T(8,128)(2,1)S(1)}, bf16[128,576]{1,0:T(8,128)(2,1)S(1)}, u32[]{:S(2)}, u32[]{:S(2)}) collective-permute-start(bf16[128,576]{1,0:T(8,128)(2,1)S(1)} %add_convert_fusion.2), channel_id=1, source_target_pairs={{0,2},{1,3},{2,0},{3,1},{4,6},{5,7},{6,4},{7,5},{8,10},{9,11},{10,... | collective-permute-start | bytes 442376 | tf_op jit(solution)/shard_map/ppermute | solution.py:25
  81.7 10.6 %collective-permute-start.5 = (bf16[128,576]{1,0:T(8,128)(2,1)S(1)}, bf16[128,576]{1,0:T(8,128)(2,1)S(1)}, u32[]{:S(2)}, u32[]{:S(2)}) collective-permute-start(bf16[128,576]{1,0:T(8,128)(2,1)S(1)} %add_convert_fusion.1), channel_id=1, source_target_pairs={{0,4},{1,5},{2,6},{3,7},{4,0},{5,1},{6,2},{7,3},{8,12},{9,13},{10,... | collective-permute-start | bytes 442376 | tf_op jit(solution)/shard_map/ppermute | solution.py:25
where the time goes:
time: 94.3 us; the launch traced here: 93.7 us
  matrix products  33.1 us (35%)
  local copies, waits for them, and re-layouts  17 us (18%)
  waiting for transfers between devices  16.8 us (18%)
  starting transfers between devices  9.74 us (10%)
  blocking collectives  9.33 us (10%)
  other arithmetic  7.04 us (7%)
    unnamed x15, local copies, waits for them, and re-layouts  16.2 us
    ppermute x3, waiting for transfers between devices, butterfly_sum_ep(): theirs = lax.ppermute(mine, 'ep', [(i, i ^ bit) for i in range(n_ep)])  10.1 us
    all_gather x1, blocking collectives, body(): whole_keys = lax.all_gather(local_keys, 'ctx', axis=0, tiled=True)  9.33 us
    dot_general x1, matrix products, body(): jnp.einsum('shtj,sthd->jd', rounded_weights, output_grad, preferred_eleme...  6.77 us
    ppermute x3, waiting for transfers between devices, causal_reduce_ctx(): lax.ppermute(sent, 'ctx', [(i, i - shift) for i in range(shift, n_ctx)])  6.64 us
    ppermute x3, starting transfers between devices, butterfly_sum_ep(): theirs = lax.ppermute(mine, 'ep', [(i, i ^ bit) for i in range(n_ep)])  5.87 us
    dot_general x1, matrix products, body(): jnp.einsum('sthd,sjd->shtj', output_grad, whole_latent, preferred_element...  4.71 us
    dot_general x1, matrix products, body(): jnp.einsum('shtj,sthd->jd', score_grad, query_latent, preferred_element_t...  4.44 us
  transfers between devices with their start and end apart: 6, of which 4 were waited for; matrix products, arithmetic and copies ran while one was open for 17% of the time, Pallas kernels for 0%

commit v1 on v0

--- a/solution.py
+++ b/solution.py
@@ -34,7 +34,12 @@
     block_len = query_latent.shape[1]
     kvr = key_latent.shape[2]
     local_keys = jnp.concatenate([key_latent[0], key_rope[0].T], axis=1)
-    whole_keys = lax.all_gather(local_keys, "ctx", axis=0, tiled=True)
+    ring = [local_keys]
+    for hop in range(3):
+        ring.append(lax.ppermute(ring[-1], "ctx", [(dev, (dev + 1) % 4) for dev in range(4)]))
+    whole_keys = jnp.roll(
+        jnp.concatenate(ring[::-1], axis=0), (lax.axis_index("ctx") + 1) * ring[0].shape[0], axis=0
+    )
     whole_latent = whole_keys[None, :, :kvr]
     whole_rope = whole_keys[:, kvr:].T[None]
     length = whole_latent.shape[1]

time: 94.3 us -> 97.9 us (1.038)
  waiting for transfers between devices: 16.8 us -> 29.9 us
  blocking collectives: 9.33 us -> 0 us
  matrix products: 33.1 us -> 28.6 us
  starting transfers between devices: 9.74 us -> 11.9 us
  local copies, waits for them, and re-layouts: 17 us -> 19.1 us
    ppermute x0 -> x3, waiting for transfers between devices: none -> 14.4 us  [body(): lax.ppermute(ring[-1], 'ctx', [(dev, (dev + 1) % 4) for dev in range(4)])]
    all_gather x1 -> x0, blocking collectives: 9.33 us -> none  [body(): whole_keys = lax.all_gather(local_keys, 'ctx', axis=0, tiled=True)]
    unnamed x15 -> x27, local copies, waits for them, and re-layouts: 16.2 us -> 18.3 us
    dot_general x1, matrix products: 4.44 us -> 2.57 us  [body(): jnp.einsum('shtj,sthd->jd', score_grad, query_latent, preferred_element_t...]
    ppermute x3, starting transfers between devices: 5.87 us -> 7.53 us  [butterfly_sum_ep(): theirs = lax.ppermute(mine, 'ep', [(i, i ^ bit) for i in range(n_ep)])]
    dot_general x1, matrix products: 2.34 us -> 0.75 us  [body(): jnp.einsum('shtj,shdt->jd', score_grad, query_rope, preferred_element_typ...]
    convert_element_type x3, other arithmetic: 1.26 us -> 0.19 us  [butterfly_sum_ep(): mine = total.astype(jnp.bfloat16)]
    ppermute x3, waiting for transfers between devices: 10.1 us -> 9.13 us  [butterfly_sum_ep(): theirs = lax.ppermute(mine, 'ep', [(i, i ^ bit) for i in range(n_ep)])]
  transfers between devices with their start and end apart: 6 -> 9, of which waited for: 4 -> 7; matrix products, arithmetic and copies ran while one was open for 17% -> 17% of each run, Pallas kernels for 0% -> 0%
where the time goes in v1:
time: 97.9 us; the launch traced here: 97.3 us
  waiting for transfers between devices  29.9 us (31%)
  matrix products  28.6 us (29%)
  local copies, waits for them, and re-layouts  19.1 us (20%)
  starting transfers between devices  11.9 us (12%)
  other arithmetic  6.92 us (7%)
    unnamed x27, local copies, waits for them, and re-layouts  18.3 us
    ppermute x3, waiting for transfers between devices, body(): lax.ppermute(ring[-1], 'ctx', [(dev, (dev + 1) % 4) for dev in range(4)])  14.4 us
    ppermute x3, waiting for transfers between devices, butterfly_sum_ep(): theirs = lax.ppermute(mine, 'ep', [(i, i ^ bit) for i in range(n_ep)])  9.13 us
    ppermute x3, starting transfers between devices, butterfly_sum_ep(): theirs = lax.ppermute(mine, 'ep', [(i, i ^ bit) for i in range(n_ep)])  7.53 us
    ppermute x3, waiting for transfers between devices, causal_reduce_ctx(): lax.ppermute(sent, 'ctx', [(i, i - shift) for i in range(shift, n_ctx)])  6.46 us
    dot_general x1, matrix products, body(): jnp.einsum('shtj,sthd->jd', rounded_weights, output_grad, preferred_eleme...  5.8 us
    dot_general x1, matrix products, body(): jnp.einsum('sthd,sjd->shtj', output_grad, whole_latent, preferred_element...  4.42 us
    dot_general x1, matrix products, body(): jnp.einsum('shtj,sjd->sthd', score_grad, whole_latent, preferred_element_...  4.37 us
  transfers between devices with their start and end apart: 9, of which 7 were waited for; matrix products, arithmetic and copies ran while one was open for 17% of the time, Pallas kernels for 0%

profile of v1, /device:TPU:0, one launch (start us, length us, event | category | flops | bytes accessed | tf_op | source)
XLA Modules:
  0.0 97.3 jit_solution(11340428923378266741)
XLA Ops:
  0.7 1.0 %copy.27 = bf16[1,64,128]{1,2,0:T(8,128)(2,1)S(1)} copy(bf16[1,64,128]{2,1,0:T(8,128)(2,1)} %param.10) | data formatting | bytes 32768 | tf_op args[3]
  1.7 0.9 pad_maximum_fusion
  3.1 4.9 %collective-permute-done = bf16[128,576]{1,0:T(8,128)(2,1)S(1)} collective-permute-done((bf16[128,576]{1,0:T(8,128)(2,1)S(1)}, bf16[128,576]{1,0:T(8,128)(2,1)S(1)}, u32[]{:S(2)}, u32[]{:S(2)}) %collective-permute-start) | collective-permute-done | bytes 147488 | tf_op jit(solution)/shard_map/ppermute | solution.py:39
  8.0 4.7 %collective-permute-done.1 = bf16[128,576]{1,0:T(8,128)(2,1)S(1)} collective-permute-done((bf16[128,576]{1,0:T(8,128)(2,1)S(1)}, bf16[128,576]{1,0:T(8,128)(2,1)S(1)}, u32[]{:S(2)}, u32[]{:S(2)}) %collective-permute-start.1) | collective-permute-done | bytes 147488 | tf_op jit(solution)/shard_map/ppermute | solution.py:39
  12.8 4.7 %collective-permute-done.2 = bf16[128,576]{1,0:T(8,128)(2,1)S(1)} collective-permute-done((bf16[128,576]{1,0:T(8,128)(2,1)S(1)}, bf16[128,576]{1,0:T(8,128)(2,1)S(1)}, u32[]{:S(2)}, u32[]{:S(2)}) %collective-permute-start.2) | collective-permute-done | bytes 147488 | tf_op jit(solution)/shard_map/ppermute | solution.py:39
  17.6 0.9 constant_dynamic-update-slice_fusion.4
  18.7 2.9 %fusion.23 = f32[512,128,16]{1,0,2:T(8,128)S(1)} fusion(bf16[128,16,512]{2,1,0:T(8,128)(2,1)S(1)} %bitcast.145, bf16[1024,576]{1,0:T(8,128)(2,1)S(1)} %constant_dynamic-update-slice_fusion, s32[]{:T(128)S(6)} %select_n.24), kind=kOutput, calls=%fused_computation.27 | convolution fusion | flops 1073741824 | bytes 6815748 | tf_op jit(solution)/shard_map/sthd,sjd->shtj/dot_general | solution.py:49
  21.6 0.8 fusion.92
  23.0 1.3 %copy-done.1 = f32[1,16,128,512]{2,3,1,0:T(8,128)} copy-done((f32[1,16,128,512]{2,3,1,0:T(8,128)}, f32[1,16,128,512]{2,3,1,0:T(8,128)S(1)}, u32[]{:S(2)}) %copy-start.1) | copy-done | bytes 4194328
  24.3 4.1 %bitcast_convert_fusion = (f32[16,128,512]{1,2,0:T(8,128)}, bf16[512,16,128]{2,0,1:T(8,128)(2,1)}) fusion(f32[16,128]{1,0:T(8,128)S(1)} %fusion.5, f32[1,16,128,512]{2,3,1,0:T(8,128)S(1)} %get-tuple-element.31, f32[16,128]{1,0:T(8,128)S(1)} %get-tuple-element.30, bf16[1024,576]{1,0:T(8,128)(2,1)S(1)} %constant_dynamic-update-slice_fusion, s32[]{:T(128)S(6)} %select_n.24), kind=kOutput, calls=%fused_computation.18 | convolution fusion | flops 1078984704 | bytes 11026436 | tf_op jit(solution)/shard_map/shtj,sjd->sthd/dot_general | solution.py:60
  28.4 5.5 %copy.52 = f32[16,128,512]{2,0,1:T(8,128)} copy(f32[16,128,512]{1,2,0:T(8,128)} %get-tuple-element.32) | data formatting | bytes 8388608
  33.9 3.3 %multiply_reduce_fusion = f32[16,128]{0,1:T(8,128)S(1)} fusion(f32[16,128,512]{2,0,1:T(8,128)} %copy.52, bf16[1,128,16,512]{3,2,1,0:T(8,128)(2,1)} %param.11), kind=kLoop, calls=%fused_computation.6 | loop fusion | flops 3143680 | bytes 6299648
  37.3 5.8 %fusion.28 = f32[512,512]{1,0:T(8,128)S(1)} fusion(bf16[128,16,512]{2,1,0:T(8,128)(2,1)} %bitcast.147, f32[16,128]{1,0:T(8,128)S(1)} %fusion.5, f32[1,16,128,512]{2,3,1,0:T(8,128)} %copy-done.1, f32[16,128]{1,0:T(8,128)S(1)} %get-tuple-element.30), kind=kOutput, calls=%fused_computation.30 | convolution fusion | flops 1076887552 | bytes 7356416 | tf_op jit(solution)/shard_map/shtj,sthd->jd/dot_general | solution.py:81
  43.2 4.4 %fusion.1 = bf16[1,16,128,512]{2,3,1,0:T(8,128)(2,1)S(1)} fusion(f32[16,128]{1,0:T(8,128)S(1)} %copy.53, bf16[128,16,512]{2,1,0:T(8,128)(2,1)S(1)} %bitcast.148, f32[16,128]{1,0:T(8,128)S(1)} %fusion.5, f32[1,16,128,512]{2,3,1,0:T(8,128)S(1)} %copy-done.2, f32[16,128]{1,0:T(8,128)S(1)} %get-tuple-element.30, bf16[1024,576]{1,0:T(8,128)(2,1)} %copy-done.7, ...), kind=kOutput, calls=%fused_computation.2 | convolution fusion | flops 1078984704 | bytes 8937476 | tf_op jit(solution)/shard_map/sthd,sjd->shtj/dot_general | solution.py:66
  47.6 0.8 fusion.69
  48.9 2.6 %fusion.48 = bf16[512,512]{1,0:T(8,128)(2,1)S(1)} fusion(f32[512,512]{1,0:T(8,128)S(1)} %fusion.28, bf16[128,16,512]{2,1,0:T(8,128)(2,1)S(1)} %bitcast.146, bf16[1,16,128,512]{2,3,1,0:T(8,128)(2,1)S(1)} %fusion.1), kind=kOutput, calls=%fused_computation.34 | convolution fusion | flops 1074528256 | bytes 5767168 | tf_op jit(solution)/shard_map/shtj,sthd->jd/dot_general | solution.py:78
  51.6 0.8 fusion.82
  52.4 1.3 %collective-permute-start.5 = (bf16[128,576]{1,0:T(8,128)(2,1)}, bf16[128,576]{1,0:T(8,128)(2,1)S(1)}, u32[]{:S(2)}, u32[]{:S(2)}) collective-permute-start(bf16[128,576]{1,0:T(8,128)(2,1)} %get-tuple-element.29), channel_id=1, source_target_pairs={{24,0},{25,1},{26,2},{27,3},{28,4},{29,5},{30,6},{31,7}} | collective-permute-start | bytes 442376 | tf_op jit(solution)/shard_map/ppermute | solution.py:14
  53.7 1.3 %collective-permute-start.4 = (bf16[128,576]{1,0:T(8,128)(2,1)}, bf16[128,576]{1,0:T(8,128)(2,1)S(1)}, u32[]{:S(2)}, u32[]{:S(2)}) collective-permute-start(bf16[128,576]{1,0:T(8,128)(2,1)} %get-tuple-element.28), channel_id=1, source_target_pairs={{16,0},{24,8},{17,1},{25,9},{18,2},{26,10},{19,3},{27,11},{20,4},{... | collective-permute-start | bytes 442376 | tf_op jit(solution)/shard_map/ppermute | solution.py:14
  55.0 1.3 %collective-permute-start.3 = (bf16[128,576]{1,0:T(8,128)(2,1)S(1)}, bf16[128,576]{1,0:T(8,128)(2,1)S(1)}, u32[]{:S(2)}, u32[]{:S(2)}) collective-permute-start(bf16[128,576]{1,0:T(8,128)(2,1)S(1)} %get-tuple-element.27), channel_id=1, source_target_pairs={{8,0},{16,8},{24,16},{9,1},{17,9},{25,17},{10,2},{18,10},{26,18},{... | collective-permute-start | bytes 442376 | tf_op jit(solution)/shard_map/ppermute | solution.py:14
  56.3 2.9 %collective-permute-done.5 = bf16[128,576]{1,0:T(8,128)(2,1)S(1)} collective-permute-done((bf16[128,576]{1,0:T(8,128)(2,1)}, bf16[128,576]{1,0:T(8,128)(2,1)S(1)}, u32[]{:S(2)}, u32[]{:S(2)}) %collective-permute-start.5) | collective-permute-done | bytes 147488 | tf_op jit(solution)/shard_map/ppermute | solution.py:14
  59.3 3.5 %collective-permute-done.4 = bf16[128,576]{1,0:T(8,128)(2,1)S(1)} collective-permute-done((bf16[128,576]{1,0:T(8,128)(2,1)}, bf16[128,576]{1,0:T(8,128)(2,1)S(1)}, u32[]{:S(2)}, u32[]{:S(2)}) %collective-permute-start.4) | collective-permute-done | bytes 147488 | tf_op jit(solution)/shard_map/ppermute | solution.py:14
  62.9 2.4 %collective-permute-start.6 = (bf16[128,576]{1,0:T(8,128)(2,1)S(1)}, bf16[128,576]{1,0:T(8,128)(2,1)S(1)}, u32[]{:S(2)}, u32[]{:S(2)}) collective-permute-start(bf16[128,576]{1,0:T(8,128)(2,1)S(1)} %add_convert_fusion.3), channel_id=1, source_target_pairs={{0,1},{1,0},{2,3},{3,2},{4,5},{5,4},{6,7},{7,6},{8,9},{9,8},{10,11... | collective-permute-start | bytes 442376 | tf_op jit(solution)/shard_map/ppermute | solution.py:25
  65.3 4.2 %collective-permute-done.6 = bf16[128,576]{1,0:T(8,128)(2,1)S(1)} collective-permute-done((bf16[128,576]{1,0:T(8,128)(2,1)S(1)}, bf16[128,576]{1,0:T(8,128)(2,1)S(1)}, u32[]{:S(2)}, u32[]{:S(2)}) %collective-permute-start.6) | collective-permute-done | bytes 147488 | tf_op jit(solution)/shard_map/ppermute | solution.py:25
  69.5 2.5 %collective-permute-start.7 = (bf16[128,576]{1,0:T(8,128)(2,1)S(1)}, bf16[128,576]{1,0:T(8,128)(2,1)S(1)}, u32[]{:S(2)}, u32[]{:S(2)}) collective-permute-start(bf16[128,576]{1,0:T(8,128)(2,1)S(1)} %add_convert_fusion.2), channel_id=1, source_target_pairs={{0,2},{1,3},{2,0},{3,1},{4,6},{5,7},{6,4},{7,5},{8,10},{9,11},{10,... | collective-permute-start | bytes 442376 | tf_op jit(solution)/shard_map/ppermute | solution.py:25
  72.0 4.4 %fusion.25 = bf16[1,128,16,512]{1,3,2,0:T(8,128)(2,1)} fusion(bf16[1,16,128,512]{2,3,1,0:T(8,128)(2,1)} %copy-done.3, bf16[1024,576]{1,0:T(8,128)(2,1)} %copy-done.7, s32[]{:T(128)S(6)} %select_n.24), kind=kOutput, calls=%fused_computation.29 | convolution fusion | flops 1075838976 | bytes 4718596 | tf_op jit(solution)/shard_map/shtj,sjd->sthd/dot_general | solution.py:72
  76.4 4.5 %copy.41 = bf16[1,128,16,512]{3,2,1,0:T(8,128)(2,1)} copy(bf16[1,128,16,512]{1,3,2,0:T(8,128)(2,1)} %bitcast.149) | data formatting | bytes 4194304
  80.9 4.5 %copy.42 = bf16[1,128,16,512]{3,2,1,0:T(8,128)(2,1)} copy(bf16[1,128,16,512]{1,3,2,0:T(8,128)(2,1)} %fusion.25) | data formatting | bytes 4194304
  85.4 2.7 %collective-permute-start.8 = (bf16[128,576]{1,0:T(8,128)(2,1)S(1)}, bf16[128,576]{1,0:T(8,128)(2,1)S(1)}, u32[]{:S(2)}, u32[]{:S(2)}) collective-permute-start(bf16[128,576]{1,0:T(8,128)(2,1)S(1)} %add_convert_fusion.1), channel_id=1, source_target_pairs={{0,4},{1,5},{2,6},{3,7},{4,0},{5,1},{6,2},{7,3},{8,12},{9,13},{10,... | collective-permute-start | bytes 442376 | tf_op jit(solution)/shard_map/ppermute | solution.py:25
  88.1 2.9 %fusion.60 = bf16[1,16,64,128]{3,2,1,0:T(8,128)(2,1)} fusion(bf16[1,16,128,512]{2,3,1,0:T(8,128)(2,1)} %copy-done.3, bf16[1024,576]{1,0:T(8,128)(2,1)} %copy-done.7, s32[]{:T(128)S(6)} %select_n.24, s32[]{:T(128)S(6)} %add.76), kind=kOutput, calls=%fused_computation.42 | convolution fusion | flops 134479872 | bytes 2490376 | tf_op jit(solution)/shard_map/shtj,sdj->shdt/dot_general | solution.py:76
  90.9 4.9 %collective-permute-done.8 = bf16[128,576]{1,0:T(8,128)(2,1)S(1)} collective-permute-done((bf16[128,576]{1,0:T(8,128)(2,1)S(1)}, bf16[128,576]{1,0:T(8,128)(2,1)S(1)}, u32[]{:S(2)}, u32[]{:S(2)}) %collective-permute-start.8) | collective-permute-done | bytes 147488 | tf_op jit(solution)/shard_map/ppermute | solution.py:25
  96.6 0.7 copy.43
  (38 shorter events, 3.0 us)
Async XLA Ops:
  0.6 18.0 %copy-start = (bf16[1,128,16,512]{3,2,1,0:T(8,128)(2,1)S(1)}, bf16[1,128,16,512]{3,2,1,0:T(8,128)(2,1)}, u32[]{:S(2)}) copy-start(bf16[1,128,16,512]{3,2,1,0:T(8,128)(2,1)} %param.7) | copy-start | bytes 6291460
  0.6 18.0 %copy-start.5 = (bf16[1,128,512]{2,1,0:T(8,128)(2,1)S(1)}, bf16[1,128,512]{2,1,0:T(8,128)(2,1)}, u32[]{:S(2)}) copy-start(bf16[1,128,512]{2,1,0:T(8,128)(2,1)} %param.9) | copy-start | bytes 393220
  2.6 5.4 %collective-permute-start = (bf16[128,576]{1,0:T(8,128)(2,1)S(1)}, bf16[128,576]{1,0:T(8,128)(2,1)S(1)}, u32[]{:S(2)}, u32[]{:S(2)}) collective-permute-start(bf16[128,576]{1,0:T(8,128)(2,1)S(1)} %pad_maximum_fusion), channel_id=1, source_target_pairs={{0,8},{8,16},{16,24},{24,0},{1,9},{9,17},{17,25},{25,1},{2,10},{10... | collective-permute-start | bytes 442376 | tf_op jit(solution)/shard_map/ppermute | solution.py:39
  8.0 4.7 %collective-permute-start.1 = (bf16[128,576]{1,0:T(8,128)(2,1)S(1)}, bf16[128,576]{1,0:T(8,128)(2,1)S(1)}, u32[]{:S(2)}, u32[]{:S(2)}) collective-permute-start(bf16[128,576]{1,0:T(8,128)(2,1)S(1)} %collective-permute-done), channel_id=1, source_target_pairs={{0,8},{8,16},{16,24},{24,0},{1,9},{9,17},{17,25},{25,1},{2,10},{10... | collective-permute-start | bytes 442376 | tf_op jit(solution)/shard_map/ppermute | solution.py:39
  12.8 4.7 %collective-permute-start.2 = (bf16[128,576]{1,0:T(8,128)(2,1)S(1)}, bf16[128,576]{1,0:T(8,128)(2,1)S(1)}, u32[]{:S(2)}, u32[]{:S(2)}) collective-permute-start(bf16[128,576]{1,0:T(8,128)(2,1)S(1)} %collective-permute-done.1), channel_id=1, source_target_pairs={{0,8},{8,16},{16,24},{24,0},{1,9},{9,17},{17,25},{25,1},{2,10},{10... | collective-permute-start | bytes 442376 | tf_op jit(solution)/shard_map/ppermute | solution.py:39
  18.7 4.3 %copy-start.7 = (bf16[1024,576]{1,0:T(8,128)(2,1)}, bf16[1024,576]{1,0:T(8,128)(2,1)S(1)}, u32[]{:S(2)}) copy-start(bf16[1024,576]{1,0:T(8,128)(2,1)S(1)} %constant_dynamic-update-slice_fusion) | copy-start | bytes 3538948
  18.7 2.9 %copy-start.6 = (bf16[1,16,64,128]{3,2,1,0:T(8,128)(2,1)S(1)}, bf16[1,16,64,128]{3,2,1,0:T(8,128)(2,1)}, u32[]{:S(2)}) copy-start(bf16[1,16,64,128]{3,2,1,0:T(8,128)(2,1)} %param.8) | copy-start | bytes 786436
  22.4 2.0 %copy-start.1 = (f32[1,16,128,512]{2,3,1,0:T(8,128)}, f32[1,16,128,512]{2,3,1,0:T(8,128)S(1)}, u32[]{:S(2)}) copy-start(f32[1,16,128,512]{2,3,1,0:T(8,128)S(1)} %get-tuple-element.31) | copy-start | bytes 12582916
  37.3 5.8 %copy-start.2 = (f32[1,16,128,512]{2,3,1,0:T(8,128)S(1)}, f32[1,16,128,512]{2,3,1,0:T(8,128)}, u32[]{:S(2)}) copy-start(f32[1,16,128,512]{2,3,1,0:T(8,128)} %copy-done.1) | copy-start | bytes 12582916
  37.3 5.8 %copy-start.4 = (bf16[1,128,16,512]{3,2,1,0:T(8,128)(2,1)S(1)}, bf16[1,128,16,512]{3,2,1,0:T(8,128)(2,1)}, u32[]{:S(2)}) copy-start(bf16[1,128,16,512]{3,2,1,0:T(8,128)(2,1)} %param.11) | copy-start | bytes 6291460
  47.6 1.3 %copy-start.3 = (bf16[1,16,128,512]{2,3,1,0:T(8,128)(2,1)}, bf16[1,16,128,512]{2,3,1,0:T(8,128)(2,1)S(1)}, u32[]{:S(2)}) copy-start(bf16[1,16,128,512]{2,3,1,0:T(8,128)(2,1)S(1)} %fusion.1) | copy-start | bytes 6291460
  52.4 6.8 %collective-permute-start.5 = (bf16[128,576]{1,0:T(8,128)(2,1)}, bf16[128,576]{1,0:T(8,128)(2,1)S(1)}, u32[]{:S(2)}, u32[]{:S(2)}) collective-permute-start(bf16[128,576]{1,0:T(8,128)(2,1)} %get-tuple-element.29), channel_id=1, source_target_pairs={{24,0},{25,1},{26,2},{27,3},{28,4},{29,5},{30,6},{31,7}} | collective-permute-start | bytes 442376 | tf_op jit(solution)/shard_map/ppermute | solution.py:14
  53.7 9.1 %collective-permute-start.4 = (bf16[128,576]{1,0:T(8,128)(2,1)}, bf16[128,576]{1,0:T(8,128)(2,1)S(1)}, u32[]{:S(2)}, u32[]{:S(2)}) collective-permute-start(bf16[128,576]{1,0:T(8,128)(2,1)} %get-tuple-element.28), channel_id=1, source_target_pairs={{16,0},{24,8},{17,1},{25,9},{18,2},{26,10},{19,3},{27,11},{20,4},{... | collective-permute-start | bytes 442376 | tf_op jit(solution)/shard_map/ppermute | solution.py:14
  55.0 7.8 %collective-permute-start.3 = (bf16[128,576]{1,0:T(8,128)(2,1)S(1)}, bf16[128,576]{1,0:T(8,128)(2,1)S(1)}, u32[]{:S(2)}, u32[]{:S(2)}) collective-permute-start(bf16[128,576]{1,0:T(8,128)(2,1)S(1)} %get-tuple-element.27), channel_id=1, source_target_pairs={{8,0},{16,8},{24,16},{9,1},{17,9},{25,17},{10,2},{18,10},{26,18},{... | collective-permute-start | bytes 442376 | tf_op jit(solution)/shard_map/ppermute | solution.py:14
  62.9 6.6 %collective-permute-start.6 = (bf16[128,576]{1,0:T(8,128)(2,1)S(1)}, bf16[128,576]{1,0:T(8,128)(2,1)S(1)}, u32[]{:S(2)}, u32[]{:S(2)}) collective-permute-start(bf16[128,576]{1,0:T(8,128)(2,1)S(1)} %add_convert_fusion.3), channel_id=1, source_target_pairs={{0,1},{1,0},{2,3},{3,2},{4,5},{5,4},{6,7},{7,6},{8,9},{9,8},{10,11... | collective-permute-start | bytes 442376 | tf_op jit(solution)/shard_map/ppermute | solution.py:25
  69.5 15.8 %collective-permute-start.7 = (bf16[128,576]{1,0:T(8,128)(2,1)S(1)}, bf16[128,576]{1,0:T(8,128)(2,1)S(1)}, u32[]{:S(2)}, u32[]{:S(2)}) collective-permute-start(bf16[128,576]{1,0:T(8,128)(2,1)S(1)} %add_convert_fusion.2), channel_id=1, source_target_pairs={{0,2},{1,3},{2,0},{3,1},{4,6},{5,7},{6,4},{7,5},{8,10},{9,11},{10,... | collective-permute-start | bytes 442376 | tf_op jit(solution)/shard_map/ppermute | solution.py:25
  85.4 10.5 %collective-permute-start.8 = (bf16[128,576]{1,0:T(8,128)(2,1)S(1)}, bf16[128,576]{1,0:T(8,128)(2,1)S(1)}, u32[]{:S(2)}, u32[]{:S(2)}) collective-permute-start(bf16[128,576]{1,0:T(8,128)(2,1)S(1)} %add_convert_fusion.1), channel_id=1, source_target_pairs={{0,4},{1,5},{2,6},{3,7},{4,0},{5,1},{6,2},{7,3},{8,12},{9,13},{10,... | collective-permute-start | bytes 442376 | tf_op jit(solution)/shard_map/ppermute | solution.py:25
